TPU v7x, 256 devices: a whole 4x4x8 slice. The times are simulated.
256 devices in a mesh: dp: 64 (over y, z_lo, x), tensor: 4 (over z_hi, core).
Axes of the slice: x: 4, y: 4, z: 8 (z_hi: 2, z_lo: 4; z = z_hi * 4 + z_lo), core: 2. Of those that a mesh axis runs over, the one named last changes fastest.
Arguments:
- tokens: bfloat16 [16384, 8192], P('dp', 'tensor'), may hold values from -160 to 160
- weights: bfloat16 [3, 512, 32, 256], P(None, None, 'tensor'), may hold values from -0.25 to 0.25
- cotangent: bfloat16 [16384, 8192], P('dp', 'tensor'), may hold values from -6 to 6
Outputs:
- mixed: bfloat16 [16384, 8192], P('dp', 'tensor')
- token_grads: bfloat16 [16384, 8192], P('dp', 'tensor')
- weight_grads: float32 [3, 512, 32, 256], P(None, 'dp', 'tensor')
All inputs are finite; a program needn't handle non-finite values.
Results may differ from a plain program's by a relative error of at most 0.0014.
The roundings to bfloat16 on the way count: a program that leaves them out, or rounds other values in their place, can miss the bound.
Values may be sent and summed in bfloat16 or wider, within the bound.
No kernel may reach another device: no remote copies, remote signals or barrier semaphores. Data moves between devices by JAX's collectives and lax.ppermute only.
A program may use at most 128 MiB of HBM per device.

v0:
```python
import math
import jax
import jax.numpy as jnp
from jax import lax
from jax.sharding import Mesh, PartitionSpec as P

D = 8192
BLK = 256
FACTORS = 3
root_half = 0.7071067811865476
pdf_scale = 0.3989422804014327
epsilon = 1e-06


def swapped(x, axis, stride):
    return lax.ppermute(x, axis, [(i, i ^ 1 << stride) for i in range(lax.axis_size(axis))])


def tensor_sum(x):
    for bit in range(lax.axis_size("tensor").bit_length() - 1):
        x = x + swapped(x, "tensor", bit)
    return x


def scatter_first(grads):
    rows = grads.shape[0]
    ny, nz, nx = (lax.axis_size(a) for a in ("dy", "dz", "dx"))
    rest = grads.shape[1:]
    share = rows // (ny * nz * nx)
    g = lax.psum_scatter(grads.reshape(ny, -1, rest[-1]), "dy", scatter_dimension=0, tiled=True)
    return g.reshape((nz, nx, share) + rest)


def exchange_first(grads):
    rows = grads.shape[0]
    ny, nz, nx = (lax.axis_size(a) for a in ("dy", "dz", "dx"))
    rest = grads.shape[1:]
    g = grads.reshape((ny, nz, nx, rows // (ny * nz * nx)) + rest)
    return jnp.sum(lax.all_to_all(g, "dx", 2, 2), axis=2)


def scatter_rest(on_sc, on_tc):
    nz, nx, share = on_sc[0].shape[:3]
    rest = on_sc[0].shape[3:]
    a, on_tc = lax.optimization_barrier((jnp.stack(on_sc, axis=0), on_tc))
    a = jnp.moveaxis(a, 2, 0)
    a = lax.psum_scatter(a.reshape(nx, -1, rest[-1]), "dx", scatter_dimension=0, tiled=True)
    a = a.reshape((len(on_sc), nz, share) + rest)
    b = jnp.sum(lax.all_to_all(on_tc, "dy", 0, 0), axis=0)
    g = jnp.moveaxis(jnp.concatenate([b[None], a], axis=0), 1, 0)
    return jnp.sum(lax.all_to_all(g, "dz", 0, 0), axis=0)


def partner_rows(rows):
    pieces = lax.axis_size(("dy", "dx"))
    piece = rows.shape[0] // pieces
    mine = lax.axis_index("dy") * lax.axis_size("dx") + lax.axis_index("dx")
    part = lax.dynamic_slice_in_dim(rows, mine * piece, piece, axis=0)
    part = swapped(part, "tensor", 1)
    return lax.all_gather(part, ("dy", "dx"), axis=0, tiled=True)


def gelu_value(value):
    return value * (0.5 * (1.0 + lax.erf(value * root_half)))


def gelu_slope(value):
    return (
        0.5 * (1.0 + lax.erf(value * root_half)) + value * jnp.exp(-0.5 * value * value) * pdf_scale
    )


def local_partner(blocks, stride):
    tok_rows, block_count, width = blocks.shape
    folded = blocks.reshape(tok_rows, block_count // (2 * stride), 2, stride, width)
    return jnp.flip(folded, axis=2).reshape(tok_rows, block_count, width)


def apply_factor(hidden, partner, layer_weights):
    preact = jnp.einsum(
        "tbc,cbd->tbd", hidden, layer_weights[:BLK], preferred_element_type=jnp.float32
    )
    return preact + jnp.einsum(
        "tbc,cbd->tbd", partner, layer_weights[BLK:], preferred_element_type=jnp.float32
    )


def shards(tokens, weights, cotangent):
    tok_rows, local_width = tokens.shape
    blocks_dev = local_width // BLK
    block_bits = (D // BLK).bit_length() - 1
    device_bits = blocks_dev.bit_length() - 1
    data_size = lax.axis_size(("dy", "dz", "dx"))
    grad_scale = 1.0 / math.sqrt(tok_rows * data_size)
    top = FACTORS - 1
    assert block_bits - 1 - device_bits == 1
    cot_blocks = cotangent.reshape(tok_rows, blocks_dev, BLK)
    partner_cot = swapped(cot_blocks, "tensor", 1)
    tokens_f32 = tokens.astype(jnp.float32)
    square_sum = tensor_sum(jnp.sum(tokens_f32 * tokens_f32, axis=1))
    inv_rms = lax.rsqrt(square_sum / D + epsilon)[:, None]
    normed = tokens_f32 * inv_rms
    hidden = normed.astype(jnp.bfloat16).reshape(tok_rows, blocks_dev, BLK)
    stored_inputs = []
    stored_preact = []
    for factor in range(top):
        bit_index = block_bits - FACTORS + factor
        stride = 1 << bit_index
        if stride < blocks_dev:
            partner = local_partner(hidden, stride)
        else:
            partner = swapped(hidden, "tensor", bit_index - device_bits)
        preact = apply_factor(hidden, partner, weights[factor])
        stored_inputs.append((hidden, partner))
        stored_preact.append(preact)
        hidden = gelu_value(preact).astype(jnp.bfloat16)
    hidden, partner_cot = lax.optimization_barrier((hidden, partner_cot))
    partner_top = swapped(hidden, "tensor", 1)
    top_weights = weights[top]
    grad_hidden = jnp.einsum(
        "tbd,cbd->tbc", cot_blocks, top_weights[:BLK], preferred_element_type=jnp.float32
    ) + jnp.einsum(
        "tbd,cbd->tbc",
        partner_cot,
        partner_rows(top_weights[BLK:]),
        preferred_element_type=jnp.float32,
    )
    grad_pre = (grad_hidden * gelu_slope(stored_preact[top - 1])).astype(jnp.bfloat16)
    grad_terms = [None] * FACTORS
    for factor in reversed(range(top)):
        bit_index = block_bits - FACTORS + factor
        stride = 1 << bit_index
        kept_hidden, kept_partner = stored_inputs[factor]
        joined = jnp.concatenate([kept_hidden, kept_partner], axis=2)
        grad_terms[factor] = (exchange_first if factor == 0 else scatter_first)(
            jnp.einsum("tbc,tbd->cbd", joined, grad_pre, preferred_element_type=jnp.float32)
            * grad_scale
        )
        layer_weights = weights[factor]
        near_term = jnp.einsum(
            "tbd,cbd->tbc", grad_pre, layer_weights[:BLK], preferred_element_type=jnp.float32
        )
        far_term = jnp.einsum(
            "tbd,cbd->tbc", grad_pre, layer_weights[BLK:], preferred_element_type=jnp.float32
        )
        if stride < blocks_dev:
            arrived = local_partner(far_term, stride)
        else:
            arrived = swapped(far_term, "tensor", bit_index - device_bits)
        grad_hidden = near_term + arrived
        if factor > 0:
            previous = stored_preact[factor - 1]
            grad_pre = (grad_hidden * gelu_slope(previous)).astype(jnp.bfloat16)
    partner_top, _ = lax.optimization_barrier((partner_top, grad_hidden))
    preact = apply_factor(hidden, partner_top, top_weights)
    mixed = (tokens_f32 + preact.reshape(tok_rows, local_width)).astype(jnp.bfloat16)
    joined = jnp.concatenate([hidden, partner_top], axis=2)
    grad_terms[top] = scatter_first(
        jnp.einsum("tbc,tbd->cbd", joined, cot_blocks, preferred_element_type=jnp.float32)
        * grad_scale
    )
    flat = grad_hidden.reshape(tok_rows, local_width)
    inner_sum = tensor_sum(jnp.sum(flat * normed, axis=1))
    token_grads = (
        cotangent.astype(jnp.float32) + inv_rms * (flat - normed * (inner_sum / D)[:, None])
    ).astype(jnp.bfloat16)
    weight_grads = scatter_rest(grad_terms[1:], grad_terms[0])
    return (mixed, token_grads, weight_grads)


def solution(mesh):
    ny, nz, nx = (4, 4, 4)
    fine = Mesh(
        mesh.devices.reshape(ny, nz, nx, mesh.shape["tensor"]), ("dy", "dz", "dx", "tensor")
    )
    dp = ("dy", "dz", "dx")
    return jax.shard_map(
        shards,
        mesh=fine,
        in_specs=(P(dp, "tensor"), P(None, None, "tensor", None), P(dp, "tensor")),
        out_specs=(P(dp, "tensor"), P(dp, "tensor"), P(None, dp, "tensor", None)),
        check_vma=False,
    )
```

profile of v0, /device:TPU:1, one launch (start us, length us, event | category | flops | bytes accessed | tf_op | source)
XLA Modules:
  0.0 300.6 jit_solution(10783310645281897651)
XLA Ops:
  9.0 3.3 %collective-permute-start = (f32[256]{0:T(256)S(1)}, f32[256]{0:T(256)S(1)}, u32[]{:S(2)}, u32[]{:S(2)}) collective-permute-start(f32[256]{0:T(256)S(1)} %fusion.8), channel_id=1, source_target_pairs={{0,1},{1,0},{2,3},{3,2},{4,5},{5,4},{6,7},{7,6},{8,9},{9,8},{10,11... | collective-permute-start | bytes 3080 | tf_op jit(solution)/shard_map/ppermute | solution.py:16
  12.3 5.2 %fusion.54 = (bf16[1,256,8,256]{3,2,1,0:T(8,128)(2,1)}, bf16[1,256,8,256]{3,2,1,0:T(8,128)(2,1)}, bf16[1,256,8,256]{3,2,1,0:T(8,128)(2,1)}, bf16[1,256,8,256]{3,...) fusion(bf16[3,512,8,256]{3,2,1,0:T(8,128)(2,1)} %param.4), kind=kLoop, calls=%fused_computation.80 | loop fusion | bytes 12582912 | tf_op jit(solution)/shard_map/slice | solution.py:84
  19.2 5.3 %collective-permute-start.1 = (f32[256]{0:T(256)S(1)}, f32[256]{0:T(256)S(1)}, u32[]{:S(2)}, u32[]{:S(2)}) collective-permute-start(f32[256]{0:T(256)S(1)} %add.80), channel_id=1, source_target_pairs={{0,2},{1,3},{2,0},{3,1},{4,6},{5,7},{6,4},{7,5},{8,10},{9,11},{10,... | collective-permute-start | bytes 3080 | tf_op jit(solution)/shard_map/ppermute | solution.py:16
  41.2 4.4 %collective-permute-start.3 = (bf16[256,8,256]{2,0,1:T(8,128)(2,1)}, bf16[256,8,256]{2,0,1:T(8,128)(2,1)}, u32[]{:S(2)}, u32[]{:S(2)}) collective-permute-start(bf16[256,8,256]{2,0,1:T(8,128)(2,1)} %bitcast.127), channel_id=1, source_target_pairs={{0,2},{1,3},{2,0},{3,1},{4,6},{5,7},{6,4},{7,5},{8,10},{9,11},{10,... | collective-permute-start | bytes 3145736 | tf_op jit(solution)/shard_map/ppermute | solution.py:16
  51.1 3.7 %fusion.34 = (bf16[256,8,256]{0,2,1:T(8,128)(2,1)}, f32[8,256,256]{1,2,0:T(8,128)}) fusion(f32[8,256,256]{1,2,0:T(8,128)S(1)} %fusion.50, bf16[256,8,256]{0,2,1:T(8,128)(2,1)} %collective-permute-done.2, bf16[1,256,8,256]{3,2,1,0:T(8,128)(2,1)S(1)} %copy-done.3), kind=kOutput, calls=%fused_computation.47 | convolution fusion | flops 271581184 | bytes 7340032 | tf_op jit(solution)/shard_map/tbc,cbd->tbd/dot_general | solution.py:83
  54.8 21.4 %collective-permute-done.3 = bf16[256,8,256]{2,0,1:T(8,128)(2,1)} collective-permute-done((bf16[256,8,256]{2,0,1:T(8,128)(2,1)}, bf16[256,8,256]{2,0,1:T(8,128)(2,1)}, u32[]{:S(2)}, u32[]{:S(2)}) %collective-permute-start.3) | collective-permute-done | bytes 1048608 | tf_op jit(solution)/shard_map/ppermute | solution.py:16
  76.2 6.7 %all-gather.2.cloned.1.call-done = bf16[256,8,256]{2,0,1:T(8,128)(2,1)} async-done(((bf16[16,8,256]{2,0,1:T(8,128)(2,1)}), bf16[256,8,256]{2,0,1:T(8,128)(2,1)}) %all-gather.2.cloned.1.call-update) | async-done | bytes 1048592 | tf_op jit(solution)/shard_map/all_gather | solution.py:60
  82.9 4.0 %fusion.15 = bf16[256,8,256]{0,2,1:T(8,128)(2,1)S(1)} fusion(f32[8,256,256]{1,2,0:T(8,128)} %get-tuple-element.33, f32[8,256,256]{2,1,0:T(8,128)} %fusion.41, bf16[256,8,256]{2,0,1:T(8,128)(2,1)} %all-gather.2.cloned.1.call-done, bf16[256,8,256]{2,0,1:T(8,128)(2,1)} %collective-permute-done.3), kind=kOutput, calls=%fused_computation.23 | convolution fusion | flops 274202624 | bytes 7340032 | tf_op jit(solution)/shard_map/tbd,cbd->tbc/dot_general | solution.py:122
  87.8 4.3 %multiply_bitcast_fusion.2 = f32[512,8,256]{0,2,1:T(8,128)} fusion(bf16[256,8,256]{0,2,1:T(8,128)(2,1)S(1)} %fusion.15, bf16[256,8,256]{0,2,1:T(8,128)(2,1)} %collective-permute-done.2, bf16[256,8,256]{0,2,1:T(8,128)(2,1)} %get-tuple-element.30), kind=kOutput, calls=%fused_computation.2 | convolution fusion | flops 542113792 | bytes 7340032 | tf_op jit(solution)/shard_map/tbc,tbd->cbd/dot_general | solution.py:136
  92.1 5.4 %copy.147 = f32[512,8,256]{2,1,0:T(8,128)} copy(f32[512,8,256]{0,2,1:T(8,128)} %multiply_bitcast_fusion.2) | data formatting | bytes 8388608 | tf_op jit(solution)/shard_map/mul | solution.py:136
  101.8 5.5 %collective-permute-start.4 = (bf16[256,8,256]{0,2,1:T(8,128)(2,1)}, bf16[256,8,256]{0,2,1:T(8,128)(2,1)}, u32[]{:S(2)}, u32[]{:S(2)}) collective-permute-start(bf16[256,8,256]{0,2,1:T(8,128)(2,1)} %get-tuple-element.8), channel_id=1, source_target_pairs={{0,2},{1,3},{2,0},{3,1},{4,6},{5,7},{6,4},{7,5},{8,10},{9,11},{10,... | collective-permute-start | bytes 3145736 | tf_op jit(solution)/shard_map/ppermute | solution.py:16
  111.5 3.1 %rev.9 = f32[256,1,2,4,256]{0,4,3,2,1:T(8,128)} reverse(f32[256,1,2,4,256]{0,4,3,2,1:T(8,128)} %copy.143), dimensions={2} | reverse | bytes 4194304 | tf_op jit(solution)/shard_map/jit(_flip)/rev | solution.py:76
  117.4 13.7 %collective-permute-done.4 = bf16[256,8,256]{0,2,1:T(8,128)(2,1)} collective-permute-done((bf16[256,8,256]{0,2,1:T(8,128)(2,1)}, bf16[256,8,256]{0,2,1:T(8,128)(2,1)}, u32[]{:S(2)}, u32[]{:S(2)}) %collective-permute-start.4) | collective-permute-done | bytes 1048608 | tf_op jit(solution)/shard_map/ppermute | solution.py:16
  133.4 4.4 %copy.149 = f32[512,8,256]{2,1,0:T(8,128)} copy(f32[512,8,256]{2,0,1:T(8,128)S(1)} %multiply_bitcast_fusion.1) | data formatting | bytes 8388608 | tf_op jit(solution)/shard_map/mul | solution.py:159
  140.2 4.6 %multiply_bitcast_fusion = f32[512,8,256]{0,2,1:T(8,128)} fusion(bf16[256,8,256]{0,2,1:T(8,128)(2,1)} %copy-done.6, bf16[256,8,256]{2,0,1:T(8,128)(2,1)} %bitcast.138, bf16[256,8,256]{2,0,1:T(8,128)(2,1)} %copy.152), kind=kOutput, calls=%fused_computation | convolution fusion | flops 542113792 | bytes 7340032 | tf_op jit(solution)/shard_map/tbc,tbd->cbd/dot_general | solution.py:136
  144.7 5.4 %copy.153 = f32[512,8,256]{2,1,0:T(8,128)} copy(f32[512,8,256]{0,2,1:T(8,128)} %multiply_bitcast_fusion) | data formatting | bytes 8388608 | tf_op jit(solution)/shard_map/mul | solution.py:136
  152.8 30.1 %all_to_all.15 = f32[4,4,4,8,8,256]{5,4,3,1,0,2:T(8,128)} all-to-all(f32[4,4,4,8,8,256]{5,4,3,1,0,2:T(8,128)S(1)} %copy.154), channel_id=1, replica_groups=mesh['dy'=4,'dz'=4,'dx'=4,'tensor'=4] {'dx'}, dimensions={2} | all-to-all | bytes 8388608 | tf_op jit(solution)/shard_map/all_to_all | solution.py:39
  182.8 3.7 %reduce_sum.47 = f32[4,4,8,8,256]{4,3,2,1,0:T(8,128)} reduce(f32[4,4,4,8,8,256]{5,4,3,1,0,2:T(8,128)} %all_to_all.15, f32[]{:T(128)} %constant.7.clone.1), dimensions={2}, to_apply=%region_4.5 | reduce | flops 786432 | bytes 5242884 | tf_op jit(solution)/shard_map/reduce_sum | solution.py:39
  186.5 22.7 %reduce-scatter.6.cloned.1.call-done = f32[1,1024,256]{2,1,0:T(8,128)} async-done(((f32[4,1024,256]{2,1,0:T(8,128)}), f32[1,1024,256]{2,1,0:T(8,128)}) %reduce-scatter.6.cloned.1.call-update) | async-done | bytes 1048592 | tf_op jit(solution)/shard_map/reduce_scatter | solution.py:30
  212.4 4.3 %all-to-all-start.1 = ((f32[4,4,8,8,256]{4,3,2,1,0:T(8,128)}), f32[4,4,8,8,256]{4,3,2,1,0:T(8,128)}, u32[]{:S(2)}, u32[]{:S(2)}) async-start(f32[4,4,8,8,256]{4,3,2,1,0:T(8,128)} %reduce_sum.47), calls=%async_computation.3 | async-start | bytes 2097152 | tf_op jit(solution)/shard_map/all_to_all | solution.py:49
  223.2 5.9 %collective-permute-start.8 = (f32[256]{0:T(256)S(1)}, f32[256]{0:T(256)S(1)}, u32[]{:S(2)}, u32[]{:S(2)}) collective-permute-start(f32[256]{0:T(256)S(1)} %add.101), channel_id=1, source_target_pairs={{0,2},{1,3},{2,0},{3,1},{4,6},{5,7},{6,4},{7,5},{8,10},{9,11},{10,... | collective-permute-start | bytes 3080 | tf_op jit(solution)/shard_map/ppermute | solution.py:16
  232.4 33.5 %reduce-scatter.8.cloned.1.call-done = f32[1,512,256]{2,1,0:T(8,128)} async-done(((f32[4,512,256]{2,1,0:T(8,128)}), f32[1,512,256]{2,1,0:T(8,128)}) %reduce-scatter.8.cloned.1.call-update) | async-done | bytes 524304 | tf_op jit(solution)/shard_map/reduce_scatter | solution.py:47
  267.9 4.5 %all-to-all-start.2 = ((f32[4,3,8,8,256]{4,3,2,1,0:T(8,128)}), f32[4,3,8,8,256]{4,3,2,1,0:T(8,128)}, u32[]{:S(2)}, u32[]{:S(2)}) async-start(f32[4,3,8,8,256]{4,3,2,1,0:T(8,128)} %maximum_bitcast_fusion), calls=%async_computation.5 | async-start | bytes 1572864 | tf_op jit(solution)/shard_map/all_to_all | solution.py:51
  280.9 11.2 %all-to-all-done.2 = f32[4,3,8,8,256]{4,3,2,1,0:T(8,128)} async-done(((f32[4,3,8,8,256]{4,3,2,1,0:T(8,128)}), f32[4,3,8,8,256]{4,3,2,1,0:T(8,128)}, u32[]{:S(2)}, u32[]{:S(2)}) %all-to-all-start.2) | async-done | bytes 786464 | tf_op jit(solution)/shard_map/all_to_all | solution.py:51
  (99 shorter events, 70.1 us)
Async XLA Ops:
  7.2 75.7 %all-gather.2.cloned.1.call-start = ((), (), s32[]{:S(2)}) async-start(), calls=%async_computation.6 | async-start | bytes 1114112 | tf_op jit(solution)/shard_map/all_gather | solution.py:60
  9.0 10.2 %collective-permute-start = (f32[256]{0:T(256)S(1)}, f32[256]{0:T(256)S(1)}, u32[]{:S(2)}, u32[]{:S(2)}) collective-permute-start(f32[256]{0:T(256)S(1)} %fusion.8), channel_id=1, source_target_pairs={{0,1},{1,0},{2,3},{3,2},{4,5},{5,4},{6,7},{7,6},{8,9},{9,8},{10,11... | collective-permute-start | bytes 3080 | tf_op jit(solution)/shard_map/ppermute | solution.py:16
  19.2 11.9 %copy-start.9 = (bf16[1,256,8,256]{1,3,2,0:T(8,128)(2,1)}, bf16[1,256,8,256]{1,3,2,0:T(8,128)(2,1)S(1)}, u32[]{:S(2)}) copy-start(bf16[1,256,8,256]{1,3,2,0:T(8,128)(2,1)S(1)} %copy.182) | copy-start | bytes 3145732
  19.2 11.8 %collective-permute-start.1 = (f32[256]{0:T(256)S(1)}, f32[256]{0:T(256)S(1)}, u32[]{:S(2)}, u32[]{:S(2)}) collective-permute-start(f32[256]{0:T(256)S(1)} %add.80), channel_id=1, source_target_pairs={{0,2},{1,3},{2,0},{3,1},{4,6},{5,7},{6,4},{7,5},{8,10},{9,11},{10,... | collective-permute-start | bytes 3080 | tf_op jit(solution)/shard_map/ppermute | solution.py:16
  26.7 7.2 %collective-permute-start.5 = (bf16[16,8,256]{2,0,1:T(8,128)(2,1)S(1)}, bf16[16,8,256]{2,0,1:T(8,128)(2,1)S(1)}, u32[]{:S(2)}, u32[]{:S(2)}) collective-permute-start(bf16[16,8,256]{2,0,1:T(8,128)(2,1)S(1)} %bitcast.145), channel_id=1, source_target_pairs={{0,2},{1,3},{2,0},{3,1},{4,6},{5,7},{6,4},{7,5},{8,10},{9,11},{10,... | collective-permute-start | bytes 196616 | tf_op jit(solution)/shard_map/ppermute | solution.py:16
  31.3 5.2 %copy-start = (bf16[256,2048]{0,1:T(8,128)(2,1)}, bf16[256,2048]{0,1:T(8,128)(2,1)S(1)}, u32[]{:S(2)}) copy-start(bf16[256,2048]{0,1:T(8,128)(2,1)S(1)} %fusion.2) | copy-start | bytes 3145732
  33.9 2.6 copy-start.4
  34.6 151.9 %reduce-scatter.4.cloned.1.call-start = ((), (), s32[]{:S(2)}) async-start(), calls=%async_computation.7 | async-start | bytes 5242880 | tf_op jit(solution)/shard_map/reduce_scatter | solution.py:30
  36.5 3.6 %copy-start.1 = (bf16[256,2048]{1,0:T(8,128)(2,1)S(1)}, bf16[256,2048]{1,0:T(8,128)(2,1)}, u32[]{:S(2)}) copy-start(bf16[256,2048]{1,0:T(8,128)(2,1)} %param.5) | copy-start | bytes 3145732
  38.8 12.3 %collective-permute-start.2 = (bf16[256,8,256]{0,2,1:T(8,128)(2,1)}, bf16[256,8,256]{0,2,1:T(8,128)(2,1)}, u32[]{:S(2)}, u32[]{:S(2)}) collective-permute-start(bf16[256,8,256]{0,2,1:T(8,128)(2,1)} %get-tuple-element.30), channel_id=1, source_target_pairs={{0,1},{1,0},{2,3},{3,2},{4,5},{5,4},{6,7},{7,6},{8,9},{9,8},{10,11... | collective-permute-start | bytes 3145736 | tf_op jit(solution)/shard_map/ppermute | solution.py:16
  41.2 35.0 %collective-permute-start.3 = (bf16[256,8,256]{2,0,1:T(8,128)(2,1)}, bf16[256,8,256]{2,0,1:T(8,128)(2,1)}, u32[]{:S(2)}, u32[]{:S(2)}) collective-permute-start(bf16[256,8,256]{2,0,1:T(8,128)(2,1)} %bitcast.127), channel_id=1, source_target_pairs={{0,2},{1,3},{2,0},{3,1},{4,6},{5,7},{6,4},{7,5},{8,10},{9,11},{10,... | collective-permute-start | bytes 3145736 | tf_op jit(solution)/shard_map/ppermute | solution.py:16
  97.6 9.7 %copy-start.14 = (bf16[1,256,8,256]{3,2,1,0:T(8,128)(2,1)S(1)}, bf16[1,256,8,256]{3,2,1,0:T(8,128)(2,1)}, u32[]{:S(2)}) copy-start(bf16[1,256,8,256]{3,2,1,0:T(8,128)(2,1)} %get-tuple-element.23) | copy-start | bytes 3145732
  97.6 111.7 %reduce-scatter.6.cloned.1.call-start = ((), (), s32[]{:S(2)}) async-start(), calls=%async_computation.8 | async-start | bytes 5242880 | tf_op jit(solution)/shard_map/reduce_scatter | solution.py:30
  97.6 9.6 %copy-start.16 = (bf16[256,8,256]{0,2,1:T(8,128)(2,1)S(1)}, bf16[256,8,256]{0,2,1:T(8,128)(2,1)}, u32[]{:S(2)}) copy-start(bf16[256,8,256]{0,2,1:T(8,128)(2,1)} %copy-done.15) | copy-start | bytes 3145732
  97.7 9.6 %copy-start.17 = (f32[8,256,256]{1,2,0:T(8,128)S(1)}, f32[8,256,256]{1,2,0:T(8,128)}, u32[]{:S(2)}) copy-start(f32[8,256,256]{1,2,0:T(8,128)} %get-tuple-element.31) | copy-start | bytes 6291460
  99.5 7.8 %collective-permute-start.6 = (f32[256,8,256]{0,2,1:T(8,128)S(1)}, f32[256,8,256]{0,2,1:T(8,128)S(1)}, u32[]{:S(2)}, u32[]{:S(2)}) collective-permute-start(f32[256,8,256]{0,2,1:T(8,128)S(1)} %convolution_bitcast_fusion), channel_id=1, source_target_pairs={{0,1},{1,0},{2,3},{3,2},{4,5},{5,4},{6,7},{7,6},{8,9},{9,8},{10,11... | collective-permute-start | bytes 6291464 | tf_op jit(solution)/shard_map/ppermute | solution.py:16
  101.8 29.3 %collective-permute-start.4 = (bf16[256,8,256]{0,2,1:T(8,128)(2,1)}, bf16[256,8,256]{0,2,1:T(8,128)(2,1)}, u32[]{:S(2)}, u32[]{:S(2)}) collective-permute-start(bf16[256,8,256]{0,2,1:T(8,128)(2,1)} %get-tuple-element.8), channel_id=1, source_target_pairs={{0,2},{1,3},{2,0},{3,1},{4,6},{5,7},{6,4},{7,5},{8,10},{9,11},{10,... | collective-permute-start | bytes 3145736 | tf_op jit(solution)/shard_map/ppermute | solution.py:16
  114.6 16.5 %copy-start.2 = (bf16[256,2048]{1,0:T(8,128)(2,1)S(1)}, bf16[256,2048]{1,0:T(8,128)(2,1)}, u32[]{:S(2)}) copy-start(bf16[256,2048]{1,0:T(8,128)(2,1)} %param.5) | copy-start | bytes 3145732
  137.9 128.0 %reduce-scatter.8.cloned.1.call-start = ((), (), s32[]{:S(2)}) async-start(), calls=%async_computation.9 | async-start | bytes 2621440 | tf_op jit(solution)/shard_map/reduce_scatter | solution.py:47
  212.4 18.6 %all-to-all-start.1 = ((f32[4,4,8,8,256]{4,3,2,1,0:T(8,128)}), f32[4,4,8,8,256]{4,3,2,1,0:T(8,128)}, u32[]{:S(2)}, u32[]{:S(2)}) async-start(f32[4,4,8,8,256]{4,3,2,1,0:T(8,128)} %reduce_sum.47), calls=%async_computation.3 | async-start | bytes 2097152 | tf_op jit(solution)/shard_map/all_to_all | solution.py:49
  219.3 3.9 %collective-permute-start.7 = (f32[256]{0:T(256)S(1)}, f32[256]{0:T(256)S(1)}, u32[]{:S(2)}, u32[]{:S(2)}) collective-permute-start(f32[256]{0:T(256)S(1)} %fusion.3), channel_id=1, source_target_pairs={{0,1},{1,0},{2,3},{3,2},{4,5},{5,4},{6,7},{7,6},{8,9},{9,8},{10,11... | collective-permute-start | bytes 3080 | tf_op jit(solution)/shard_map/ppermute | solution.py:16
  223.2 51.9 %collective-permute-start.8 = (f32[256]{0:T(256)S(1)}, f32[256]{0:T(256)S(1)}, u32[]{:S(2)}, u32[]{:S(2)}) collective-permute-start(f32[256]{0:T(256)S(1)} %add.101), channel_id=1, source_target_pairs={{0,2},{1,3},{2,0},{3,1},{4,6},{5,7},{6,4},{7,5},{8,10},{9,11},{10,... | collective-permute-start | bytes 3080 | tf_op jit(solution)/shard_map/ppermute | solution.py:16
  267.9 24.3 %all-to-all-start.2 = ((f32[4,3,8,8,256]{4,3,2,1,0:T(8,128)}), f32[4,3,8,8,256]{4,3,2,1,0:T(8,128)}, u32[]{:S(2)}, u32[]{:S(2)}) async-start(f32[4,3,8,8,256]{4,3,2,1,0:T(8,128)} %maximum_bitcast_fusion), calls=%async_computation.5 | async-start | bytes 1572864 | tf_op jit(solution)/shard_map/all_to_all | solution.py:51
  272.4 2.8 copy-start.11
  (10 other events, 15.2 us)
Sparse Core Ops, SparseCore 0:
  34.8 48.0 all-gather.1
  97.7 59.3 reduce-scatter.3
  159.8 49.3 reduce-scatter.5
  212.5 53.3 reduce-scatter.7
where the time goes:
time: 302 us; the launch traced here: 301 us
  waiting for transfers between devices  111 us (37%)
  local copies, waits for them, and re-layouts  54.8 us (18%)
  matrix products  38.8 us (13%)
  starting transfers between devices  38.2 us (13%)
  blocking collectives  30.1 us (10%)
  between operations  14.1 us (5%)
  other arithmetic  13.3 us (4%)
    ppermute x9, waiting for transfers between devices, swapped(): lax.ppermute(x, axis, [(i, i ^ 1 << stride) for i in range(lax.axis_size(...  35.1 us
    reduce_scatter x1, waiting for transfers between devices, scatter_rest(): lax.psum_scatter(a.reshape(nx, -1, rest[-1]), 'dx', scatter_dimension=0,...  33.5 us
    all_to_all x1, blocking collectives, exchange_first(): return jnp.sum(lax.all_to_all(g, 'dx', 2, 2), axis=2)  30.1 us
    ppermute x9, starting transfers between devices, swapped(): lax.ppermute(x, axis, [(i, i ^ 1 << stride) for i in range(lax.axis_size(...  29.2 us
    reduce_scatter x2, waiting for transfers between devices, scatter_first(): lax.psum_scatter(grads.reshape(ny, -1, rest[-1]), 'dy', scatter_dimension...  22.7 us
    unnamed x46, local copies, waits for them, and re-layouts  17.2 us
    all_to_all x1, waiting for transfers between devices, scatter_rest(): return jnp.sum(lax.all_to_all(g, 'dz', 0, 0), axis=0)  11.2 us
    mul x2, local copies, waits for them, and re-layouts, shards(): jnp.einsum('tbc,tbd->cbd', joined, grad_pre, preferred_element_type=jnp.f...  10.9 us
  transfers between devices with their start and end apart: 15, of which 7 were waited for; matrix products, arithmetic and copies ran while one was open for 28% of the time, Pallas kernels for 0%

commit v1 on v0

--- a/solution.py
+++ b/solution.py
@@ -10,6 +10,11 @@
 root_half = 0.7071067811865476
 pdf_scale = 0.3989422804014327
 epsilon = 1e-06
+
+
+def swapped_in(block, name, dim):
+    outgoing = jnp.stack([block] * lax.axis_size(name))
+    return jnp.concatenate(lax.all_to_all(outgoing, name, 0, 0), axis=dim)
 
 
 def swapped(x, axis, stride):
@@ -57,7 +62,7 @@
     mine = lax.axis_index("dy") * lax.axis_size("dx") + lax.axis_index("dx")
     part = lax.dynamic_slice_in_dim(rows, mine * piece, piece, axis=0)
     part = swapped(part, "tensor", 1)
-    return lax.all_gather(part, ("dy", "dx"), axis=0, tiled=True)
+    return swapped_in(part, ("dy", "dx"), 0)
 
 
 def gelu_value(value):

time: 302 us -> 317 us (1.050)
  starting transfers between devices: 38.2 us -> 62.3 us
  waiting for transfers between devices: 111 us -> 92.2 us
  local copies, waits for them, and re-layouts: 54.8 us -> 60 us
  blocking collectives: 30.1 us -> 34.2 us
    ppermute x9, starting transfers between devices: 29.2 us -> 47 us  [swapped(): lax.ppermute(x, axis, [(i, i ^ 1 << stride) for i in range(lax.axis_size(...]
    reduce_scatter x2, waiting for transfers between devices: 22.7 us -> 15.9 us  [scatter_first(): lax.psum_scatter(grads.reshape(ny, -1, rest[-1]), 'dy', scatter_dimension...]
    all_gather x1 -> x0, waiting for transfers between devices: 6.66 us -> none  [partner_rows(): return lax.all_gather(part, ('dy', 'dx'), axis=0, tiled=True)]
    all_to_all x0 -> x1, starting transfers between devices: none -> 6.35 us  [swapped_in(): return jnp.concatenate(lax.all_to_all(outgoing, name, 0, 0), axis=dim)]
    all_to_all x1, blocking collectives: 30.1 us -> 34.2 us  [exchange_first(): return jnp.sum(lax.all_to_all(g, 'dx', 2, 2), axis=2)]
    unnamed x46 -> x42, local copies, waits for them, and re-layouts: 17.2 us -> 18.3 us
  transfers between devices with their start and end apart: 15 -> 15, of which waited for: 7 -> 6; matrix products, arithmetic and copies ran while one was open for 28% -> 29% of each run, Pallas kernels for 0% -> 0%
where the time goes in v1:
time: 317 us; the launch traced here: 316 us
  waiting for transfers between devices  92.2 us (29%)
  starting transfers between devices  62.3 us (20%)
  local copies, waits for them, and re-layouts  60 us (19%)
  matrix products  39.6 us (12%)
  blocking collectives  34.2 us (11%)
  between operations  14.1 us (4%)
  other arithmetic  13.3 us (4%)
    ppermute x9, starting transfers between devices, swapped(): lax.ppermute(x, axis, [(i, i ^ 1 << stride) for i in range(lax.axis_size(...  47 us
    all_to_all x1, blocking collectives, exchange_first(): return jnp.sum(lax.all_to_all(g, 'dx', 2, 2), axis=2)  34.2 us
    ppermute x9, waiting for transfers between devices, swapped(): lax.ppermute(x, axis, [(i, i ^ 1 << stride) for i in range(lax.axis_size(...  32.4 us
    reduce_scatter x1, waiting for transfers between devices, scatter_rest(): lax.psum_scatter(a.reshape(nx, -1, rest[-1]), 'dx', scatter_dimension=0,...  31.2 us
    unnamed x42, local copies, waits for them, and re-layouts  18.3 us
    reduce_scatter x2, waiting for transfers between devices, scatter_first(): lax.psum_scatter(grads.reshape(ny, -1, rest[-1]), 'dy', scatter_dimension...  15.9 us
    all_to_all x1, waiting for transfers between devices, scatter_rest(): return jnp.sum(lax.all_to_all(g, 'dz', 0, 0), axis=0)  11.2 us
    mul x2, local copies, waits for them, and re-layouts, shards(): jnp.einsum('tbc,tbd->cbd', joined, grad_pre, preferred_element_type=jnp.f...  10.9 us
  transfers between devices with their start and end apart: 15, of which 6 were waited for; matrix products, arithmetic and copies ran while one was open for 29% of the time, Pallas kernels for 0%

profile of v1, /device:TPU:1, one launch (start us, length us, event | category | flops | bytes accessed | tf_op | source)
XLA Modules:
  0.0 315.7 jit_solution(9098644054797670777)
XLA Ops:
  9.0 3.3 %collective-permute-start = (f32[256]{0:T(256)S(1)}, f32[256]{0:T(256)S(1)}, u32[]{:S(2)}, u32[]{:S(2)}) collective-permute-start(f32[256]{0:T(256)S(1)} %fusion.8), channel_id=1, source_target_pairs={{0,1},{1,0},{2,3},{3,2},{4,5},{5,4},{6,7},{7,6},{8,9},{9,8},{10,11... | collective-permute-start | bytes 3080 | tf_op jit(solution)/shard_map/ppermute | solution.py:21
  12.3 5.2 %fusion.54 = (bf16[1,256,8,256]{3,2,1,0:T(8,128)(2,1)}, bf16[1,256,8,256]{3,2,1,0:T(8,128)(2,1)}, bf16[1,256,8,256]{3,2,1,0:T(8,128)(2,1)}, bf16[1,256,8,256]{3,...) fusion(bf16[3,512,8,256]{3,2,1,0:T(8,128)(2,1)} %param.4), kind=kLoop, calls=%fused_computation.80 | loop fusion | bytes 12582912 | tf_op jit(solution)/shard_map/slice | solution.py:89
  19.2 5.3 %collective-permute-start.1 = (f32[256]{0:T(256)S(1)}, f32[256]{0:T(256)S(1)}, u32[]{:S(2)}, u32[]{:S(2)}) collective-permute-start(f32[256]{0:T(256)S(1)} %add.80), channel_id=1, source_target_pairs={{0,2},{1,3},{2,0},{3,1},{4,6},{5,7},{6,4},{7,5},{8,10},{9,11},{10,... | collective-permute-start | bytes 3080 | tf_op jit(solution)/shard_map/ppermute | solution.py:21
  41.8 6.3 %all-to-all-start = ((bf16[16,16,8,256]{3,1,2,0:T(8,128)(2,1)}), bf16[16,16,8,256]{3,1,2,0:T(8,128)(2,1)}, u32[]{:S(2)}, u32[]{:S(2)}) async-start(bf16[16,16,8,256]{3,1,2,0:T(8,128)(2,1)} %stack.4), calls=%async_computation | async-start | bytes 2097152 | tf_op jit(solution)/shard_map/all_to_all | solution.py:17
  49.3 5.6 %collective-permute-start.3 = (bf16[256,8,256]{2,0,1:T(8,128)(2,1)}, bf16[256,8,256]{2,0,1:T(8,128)(2,1)}, u32[]{:S(2)}, u32[]{:S(2)}) collective-permute-start(bf16[256,8,256]{2,0,1:T(8,128)(2,1)} %bitcast.128), channel_id=1, source_target_pairs={{0,2},{1,3},{2,0},{3,1},{4,6},{5,7},{6,4},{7,5},{8,10},{9,11},{10,... | collective-permute-start | bytes 3145736 | tf_op jit(solution)/shard_map/ppermute | solution.py:21
  70.0 14.3 %collective-permute-done.3 = bf16[256,8,256]{2,0,1:T(8,128)(2,1)} collective-permute-done((bf16[256,8,256]{2,0,1:T(8,128)(2,1)}, bf16[256,8,256]{2,0,1:T(8,128)(2,1)}, u32[]{:S(2)}, u32[]{:S(2)}) %collective-permute-start.3) | collective-permute-done | bytes 1048608 | tf_op jit(solution)/shard_map/ppermute | solution.py:21
  87.9 4.3 %multiply_bitcast_fusion.2 = f32[512,8,256]{0,2,1:T(8,128)} fusion(bf16[256,8,256]{0,2,1:T(8,128)(2,1)S(1)} %fusion.15, bf16[256,8,256]{0,2,1:T(8,128)(2,1)} %collective-permute-done.2, bf16[256,8,256]{0,2,1:T(8,128)(2,1)} %get-tuple-element.30), kind=kOutput, calls=%fused_computation.2 | convolution fusion | flops 542113792 | bytes 7340032 | tf_op jit(solution)/shard_map/tbc,tbd->cbd/dot_general | solution.py:141
  92.2 5.4 %copy.151 = f32[512,8,256]{2,1,0:T(8,128)} copy(f32[512,8,256]{0,2,1:T(8,128)} %multiply_bitcast_fusion.2) | data formatting | bytes 8388608 | tf_op jit(solution)/shard_map/mul | solution.py:141
  99.6 16.5 %collective-permute-start.6 = (f32[256,8,256]{0,2,1:T(8,128)S(1)}, f32[256,8,256]{0,2,1:T(8,128)S(1)}, u32[]{:S(2)}, u32[]{:S(2)}) collective-permute-start(f32[256,8,256]{0,2,1:T(8,128)S(1)} %convolution_bitcast_fusion), channel_id=1, source_target_pairs={{0,1},{1,0},{2,3},{3,2},{4,5},{5,4},{6,7},{7,6},{8,9},{9,8},{10,11... | collective-permute-start | bytes 6291464 | tf_op jit(solution)/shard_map/ppermute | solution.py:21
  116.1 6.2 %collective-permute-start.4 = (bf16[256,8,256]{0,2,1:T(8,128)(2,1)}, bf16[256,8,256]{0,2,1:T(8,128)(2,1)}, u32[]{:S(2)}, u32[]{:S(2)}) collective-permute-start(bf16[256,8,256]{0,2,1:T(8,128)(2,1)} %get-tuple-element.8), channel_id=1, source_target_pairs={{0,2},{1,3},{2,0},{3,1},{4,6},{5,7},{6,4},{7,5},{8,10},{9,11},{10,... | collective-permute-start | bytes 3145736 | tf_op jit(solution)/shard_map/ppermute | solution.py:21
  126.5 3.6 %rev.9 = f32[256,1,2,4,256]{0,4,3,2,1:T(8,128)} reverse(f32[256,1,2,4,256]{0,4,3,2,1:T(8,128)} %copy.147), dimensions={2} | reverse | bytes 4194304 | tf_op jit(solution)/shard_map/jit(_flip)/rev | solution.py:81
  132.9 18.0 %collective-permute-done.4 = bf16[256,8,256]{0,2,1:T(8,128)(2,1)} collective-permute-done((bf16[256,8,256]{0,2,1:T(8,128)(2,1)}, bf16[256,8,256]{0,2,1:T(8,128)(2,1)}, u32[]{:S(2)}, u32[]{:S(2)}) %collective-permute-start.4) | collective-permute-done | bytes 1048608 | tf_op jit(solution)/shard_map/ppermute | solution.py:21
  153.2 4.4 %copy.153 = f32[512,8,256]{2,1,0:T(8,128)} copy(f32[512,8,256]{2,0,1:T(8,128)S(1)} %multiply_bitcast_fusion.1) | data formatting | bytes 8388608 | tf_op jit(solution)/shard_map/mul | solution.py:164
  160.0 4.5 %multiply_bitcast_fusion = f32[512,8,256]{0,2,1:T(8,128)} fusion(bf16[256,8,256]{0,2,1:T(8,128)(2,1)} %copy-done.4, bf16[256,8,256]{2,0,1:T(8,128)(2,1)} %bitcast.139, bf16[256,8,256]{2,0,1:T(8,128)(2,1)} %copy.156), kind=kOutput, calls=%fused_computation | convolution fusion | flops 542113792 | bytes 7340032 | tf_op jit(solution)/shard_map/tbc,tbd->cbd/dot_general | solution.py:141
  164.5 5.5 %copy.157 = f32[512,8,256]{2,1,0:T(8,128)} copy(f32[512,8,256]{0,2,1:T(8,128)} %multiply_bitcast_fusion) | data formatting | bytes 8388608 | tf_op jit(solution)/shard_map/mul | solution.py:141
  172.5 34.2 %all_to_all.20 = f32[4,4,4,8,8,256]{5,4,3,1,0,2:T(8,128)} all-to-all(f32[4,4,4,8,8,256]{5,4,3,1,0,2:T(8,128)S(1)} %copy.158), channel_id=1, replica_groups=mesh['dy'=4,'dz'=4,'dx'=4,'tensor'=4] {'dx'}, dimensions={2} | all-to-all | bytes 8388608 | tf_op jit(solution)/shard_map/all_to_all | solution.py:44
  206.7 3.6 %reduce_sum.47 = f32[4,4,8,8,256]{4,3,2,1,0:T(8,128)} reduce(f32[4,4,4,8,8,256]{5,4,3,1,0,2:T(8,128)} %all_to_all.20, f32[]{:T(128)} %constant.7.clone.1), dimensions={2}, to_apply=%region_4.5 | reduce | flops 786432 | bytes 5242884 | tf_op jit(solution)/shard_map/reduce_sum | solution.py:44
  210.3 15.9 %reduce-scatter.6.cloned.1.call-done = f32[1,1024,256]{2,1,0:T(8,128)} async-done(((f32[4,1024,256]{2,1,0:T(8,128)}), f32[1,1024,256]{2,1,0:T(8,128)}) %reduce-scatter.6.cloned.1.call-update) | async-done | bytes 1048592 | tf_op jit(solution)/shard_map/reduce_scatter | solution.py:35
  229.3 4.3 %all-to-all-start.2 = ((f32[4,4,8,8,256]{4,3,2,1,0:T(8,128)}), f32[4,4,8,8,256]{4,3,2,1,0:T(8,128)}, u32[]{:S(2)}, u32[]{:S(2)}) async-start(f32[4,4,8,8,256]{4,3,2,1,0:T(8,128)} %reduce_sum.47), calls=%async_computation.4 | async-start | bytes 2097152 | tf_op jit(solution)/shard_map/all_to_all | solution.py:54
  236.2 3.7 %collective-permute-start.7 = (f32[256]{0:T(256)S(1)}, f32[256]{0:T(256)S(1)}, u32[]{:S(2)}, u32[]{:S(2)}) collective-permute-start(f32[256]{0:T(256)S(1)} %fusion.3), channel_id=1, source_target_pairs={{0,1},{1,0},{2,3},{3,2},{4,5},{5,4},{6,7},{7,6},{8,9},{9,8},{10,11... | collective-permute-start | bytes 3080 | tf_op jit(solution)/shard_map/ppermute | solution.py:21
  243.0 5.5 %collective-permute-start.8 = (f32[256]{0:T(256)S(1)}, f32[256]{0:T(256)S(1)}, u32[]{:S(2)}, u32[]{:S(2)}) collective-permute-start(f32[256]{0:T(256)S(1)} %add.101), channel_id=1, source_target_pairs={{0,2},{1,3},{2,0},{3,1},{4,6},{5,7},{6,4},{7,5},{8,10},{9,11},{10,... | collective-permute-start | bytes 3080 | tf_op jit(solution)/shard_map/ppermute | solution.py:21
  249.8 31.2 %reduce-scatter.8.cloned.1.call-done = f32[1,512,256]{2,1,0:T(8,128)} async-done(((f32[4,512,256]{2,1,0:T(8,128)}), f32[1,512,256]{2,1,0:T(8,128)}) %reduce-scatter.8.cloned.1.call-update) | async-done | bytes 524304 | tf_op jit(solution)/shard_map/reduce_scatter | solution.py:52
  283.0 4.5 %all-to-all-start.3 = ((f32[4,3,8,8,256]{4,3,2,1,0:T(8,128)}), f32[4,3,8,8,256]{4,3,2,1,0:T(8,128)}, u32[]{:S(2)}, u32[]{:S(2)}) async-start(f32[4,3,8,8,256]{4,3,2,1,0:T(8,128)} %maximum_bitcast_fusion), calls=%async_computation.6 | async-start | bytes 1572864 | tf_op jit(solution)/shard_map/all_to_all | solution.py:56
  296.0 11.2 %all-to-all-done.3 = f32[4,3,8,8,256]{4,3,2,1,0:T(8,128)} async-done(((f32[4,3,8,8,256]{4,3,2,1,0:T(8,128)}), f32[4,3,8,8,256]{4,3,2,1,0:T(8,128)}, u32[]{:S(2)}, u32[]{:S(2)}) %all-to-all-start.3) | async-done | bytes 786464 | tf_op jit(solution)/shard_map/all_to_all | solution.py:56
  (97 shorter events, 78.9 us)
Async XLA Ops:
  9.0 10.2 %collective-permute-start = (f32[256]{0:T(256)S(1)}, f32[256]{0:T(256)S(1)}, u32[]{:S(2)}, u32[]{:S(2)}) collective-permute-start(f32[256]{0:T(256)S(1)} %fusion.8), channel_id=1, source_target_pairs={{0,1},{1,0},{2,3},{3,2},{4,5},{5,4},{6,7},{7,6},{8,9},{9,8},{10,11... | collective-permute-start | bytes 3080 | tf_op jit(solution)/shard_map/ppermute | solution.py:21
  19.1 12.7 %copy-start.7 = (bf16[1,256,8,256]{1,3,2,0:T(8,128)(2,1)}, bf16[1,256,8,256]{1,3,2,0:T(8,128)(2,1)S(1)}, u32[]{:S(2)}) copy-start(bf16[1,256,8,256]{1,3,2,0:T(8,128)(2,1)S(1)} %copy.186) | copy-start | bytes 3145732
  19.2 12.7 %collective-permute-start.1 = (f32[256]{0:T(256)S(1)}, f32[256]{0:T(256)S(1)}, u32[]{:S(2)}, u32[]{:S(2)}) collective-permute-start(f32[256]{0:T(256)S(1)} %add.80), channel_id=1, source_target_pairs={{0,2},{1,3},{2,0},{3,1},{4,6},{5,7},{6,4},{7,5},{8,10},{9,11},{10,... | collective-permute-start | bytes 3080 | tf_op jit(solution)/shard_map/ppermute | solution.py:21
  26.7 14.0 %collective-permute-start.5 = (bf16[16,8,256]{2,1,0:T(8,128)(2,1)S(1)}, bf16[16,8,256]{2,1,0:T(8,128)(2,1)S(1)}, u32[]{:S(2)}, u32[]{:S(2)}) collective-permute-start(bf16[16,8,256]{2,1,0:T(8,128)(2,1)S(1)} %bitcast.147), channel_id=1, source_target_pairs={{0,2},{1,3},{2,0},{3,1},{4,6},{5,7},{6,4},{7,5},{8,10},{9,11},{10,... | collective-permute-start | bytes 196616 | tf_op jit(solution)/shard_map/ppermute | solution.py:21
  32.0 5.7 %copy-start = (bf16[256,2048]{0,1:T(8,128)(2,1)}, bf16[256,2048]{0,1:T(8,128)(2,1)S(1)}, u32[]{:S(2)}) copy-start(bf16[256,2048]{0,1:T(8,128)(2,1)S(1)} %fusion.2) | copy-start | bytes 3145732
  40.0 8.2 %copy-start.1 = (bf16[256,2048]{1,0:T(8,128)(2,1)S(1)}, bf16[256,2048]{1,0:T(8,128)(2,1)}, u32[]{:S(2)}) copy-start(bf16[256,2048]{1,0:T(8,128)(2,1)} %param.5) | copy-start | bytes 3145732
  40.1 26.4 %collective-permute-start.2 = (bf16[256,8,256]{0,2,1:T(8,128)(2,1)}, bf16[256,8,256]{0,2,1:T(8,128)(2,1)}, u32[]{:S(2)}, u32[]{:S(2)}) collective-permute-start(bf16[256,8,256]{0,2,1:T(8,128)(2,1)} %get-tuple-element.30), channel_id=1, source_target_pairs={{0,1},{1,0},{2,3},{3,2},{4,5},{5,4},{6,7},{7,6},{8,9},{9,8},{10,11... | collective-permute-start | bytes 3145736 | tf_op jit(solution)/shard_map/ppermute | solution.py:21
  41.8 23.1 %all-to-all-start = ((bf16[16,16,8,256]{3,1,2,0:T(8,128)(2,1)}), bf16[16,16,8,256]{3,1,2,0:T(8,128)(2,1)}, u32[]{:S(2)}, u32[]{:S(2)}) async-start(bf16[16,16,8,256]{3,1,2,0:T(8,128)(2,1)} %stack.4), calls=%async_computation | async-start | bytes 2097152 | tf_op jit(solution)/shard_map/all_to_all | solution.py:17
  48.2 162.1 %reduce-scatter.4.cloned.1.call-start = ((), (), s32[]{:S(2)}) async-start(), calls=%async_computation.7 | async-start | bytes 5242880 | tf_op jit(solution)/shard_map/reduce_scatter | solution.py:35
  49.3 35.0 %collective-permute-start.3 = (bf16[256,8,256]{2,0,1:T(8,128)(2,1)}, bf16[256,8,256]{2,0,1:T(8,128)(2,1)}, u32[]{:S(2)}, u32[]{:S(2)}) collective-permute-start(bf16[256,8,256]{2,0,1:T(8,128)(2,1)} %bitcast.128), channel_id=1, source_target_pairs={{0,2},{1,3},{2,0},{3,1},{4,6},{5,7},{6,4},{7,5},{8,10},{9,11},{10,... | collective-permute-start | bytes 3145736 | tf_op jit(solution)/shard_map/ppermute | solution.py:21
  66.9 17.5 %copy-start.16 = (f32[8,256,256]{2,1,0:T(8,128)S(1)}, f32[8,256,256]{2,1,0:T(8,128)}, u32[]{:S(2)}) copy-start(f32[8,256,256]{2,1,0:T(8,128)} %fusion.41) | copy-start | bytes 6291460
  97.7 24.6 %copy-start.12 = (bf16[1,256,8,256]{3,2,1,0:T(8,128)(2,1)S(1)}, bf16[1,256,8,256]{3,2,1,0:T(8,128)(2,1)}, u32[]{:S(2)}) copy-start(bf16[1,256,8,256]{3,2,1,0:T(8,128)(2,1)} %get-tuple-element.23) | copy-start | bytes 3145732
  97.7 128.5 %reduce-scatter.6.cloned.1.call-start = ((), (), s32[]{:S(2)}) async-start(), calls=%async_computation.8 | async-start | bytes 5242880 | tf_op jit(solution)/shard_map/reduce_scatter | solution.py:35
  97.7 24.5 %copy-start.14 = (bf16[256,8,256]{0,2,1:T(8,128)(2,1)S(1)}, bf16[256,8,256]{0,2,1:T(8,128)(2,1)}, u32[]{:S(2)}) copy-start(bf16[256,8,256]{0,2,1:T(8,128)(2,1)} %copy-done.13) | copy-start | bytes 3145732
  97.7 24.5 %copy-start.15 = (f32[8,256,256]{1,2,0:T(8,128)S(1)}, f32[8,256,256]{1,2,0:T(8,128)}, u32[]{:S(2)}) copy-start(f32[8,256,256]{1,2,0:T(8,128)} %get-tuple-element.31) | copy-start | bytes 6291460
  99.6 22.7 %collective-permute-start.6 = (f32[256,8,256]{0,2,1:T(8,128)S(1)}, f32[256,8,256]{0,2,1:T(8,128)S(1)}, u32[]{:S(2)}, u32[]{:S(2)}) collective-permute-start(f32[256,8,256]{0,2,1:T(8,128)S(1)} %convolution_bitcast_fusion), channel_id=1, source_target_pairs={{0,1},{1,0},{2,3},{3,2},{4,5},{5,4},{6,7},{7,6},{8,9},{9,8},{10,11... | collective-permute-start | bytes 6291464 | tf_op jit(solution)/shard_map/ppermute | solution.py:21
  116.1 34.9 %collective-permute-start.4 = (bf16[256,8,256]{0,2,1:T(8,128)(2,1)}, bf16[256,8,256]{0,2,1:T(8,128)(2,1)}, u32[]{:S(2)}, u32[]{:S(2)}) collective-permute-start(bf16[256,8,256]{0,2,1:T(8,128)(2,1)} %get-tuple-element.8), channel_id=1, source_target_pairs={{0,2},{1,3},{2,0},{3,1},{4,6},{5,7},{6,4},{7,5},{8,10},{9,11},{10,... | collective-permute-start | bytes 3145736 | tf_op jit(solution)/shard_map/ppermute | solution.py:21
  130.1 20.9 %copy-start.2 = (bf16[256,2048]{1,0:T(8,128)(2,1)S(1)}, bf16[256,2048]{1,0:T(8,128)(2,1)}, u32[]{:S(2)}) copy-start(bf16[256,2048]{1,0:T(8,128)(2,1)} %param.5) | copy-start | bytes 3145732
  157.7 123.3 %reduce-scatter.8.cloned.1.call-start = ((), (), s32[]{:S(2)}) async-start(), calls=%async_computation.9 | async-start | bytes 2621440 | tf_op jit(solution)/shard_map/reduce_scatter | solution.py:52
  229.3 19.1 %all-to-all-start.2 = ((f32[4,4,8,8,256]{4,3,2,1,0:T(8,128)}), f32[4,4,8,8,256]{4,3,2,1,0:T(8,128)}, u32[]{:S(2)}, u32[]{:S(2)}) async-start(f32[4,4,8,8,256]{4,3,2,1,0:T(8,128)} %reduce_sum.47), calls=%async_computation.4 | async-start | bytes 2097152 | tf_op jit(solution)/shard_map/all_to_all | solution.py:54
  235.9 4.1 %copy-start.8 = (bf16[1,256,8,256]{1,3,2,0:T(8,128)(2,1)S(1)}, bf16[1,256,8,256]{1,3,2,0:T(8,128)(2,1)}, u32[]{:S(2)}) copy-start(bf16[1,256,8,256]{1,3,2,0:T(8,128)(2,1)} %copy-done.7) | copy-start | bytes 3145732
  236.2 6.7 %collective-permute-start.7 = (f32[256]{0:T(256)S(1)}, f32[256]{0:T(256)S(1)}, u32[]{:S(2)}, u32[]{:S(2)}) collective-permute-start(f32[256]{0:T(256)S(1)} %fusion.3), channel_id=1, source_target_pairs={{0,1},{1,0},{2,3},{3,2},{4,5},{5,4},{6,7},{7,6},{8,9},{9,8},{10,11... | collective-permute-start | bytes 3080 | tf_op jit(solution)/shard_map/ppermute | solution.py:21
  243.0 47.3 %collective-permute-start.8 = (f32[256]{0:T(256)S(1)}, f32[256]{0:T(256)S(1)}, u32[]{:S(2)}, u32[]{:S(2)}) collective-permute-start(f32[256]{0:T(256)S(1)} %add.101), channel_id=1, source_target_pairs={{0,2},{1,3},{2,0},{3,1},{4,6},{5,7},{6,4},{7,5},{8,10},{9,11},{10,... | collective-permute-start | bytes 3080 | tf_op jit(solution)/shard_map/ppermute | solution.py:21
  283.0 24.3 %all-to-all-start.3 = ((f32[4,3,8,8,256]{4,3,2,1,0:T(8,128)}), f32[4,3,8,8,256]{4,3,2,1,0:T(8,128)}, u32[]{:S(2)}, u32[]{:S(2)}) async-start(f32[4,3,8,8,256]{4,3,2,1,0:T(8,128)} %maximum_bitcast_fusion), calls=%async_computation.6 | async-start | bytes 1572864 | tf_op jit(solution)/shard_map/all_to_all | solution.py:56
  (8 other events, 15.6 us)
Sparse Core Ops, SparseCore 0:
  97.8 67.1 reduce-scatter.3
  167.7 58.4 reduce-scatter.5
  229.5 51.4 reduce-scatter.7
